TPU v7x, 256 devices: a whole 4x4x8 slice. The times are simulated.
256 devices in a mesh: seq: 32 (over x, z), ch: 8 (over y, core).
Axes of the slice: x: 4, y: 4, z: 8, core: 2. Of those that a mesh axis runs over, the one named last changes fastest.
Arguments:
- residual_in: bfloat16 [4096, 32768], P('ch', 'seq'), may hold values from -60 to 60
- key_value: bfloat16 [4096, 32768], P('ch', 'seq'), may hold values from -6 to 6
- query_gate: bfloat16 [4096, 32768], P('ch', 'seq'), may hold values from -6 to 6
- decay_rates: float32 [4096, 16], P('ch'), may hold values from 1 to 1024, as said below
- residues: float32 [4096, 16], P('ch'), may hold values from -1.8 to 1.8
- out_weight: bfloat16 [4096, 4096], P('ch'), may hold values from -0.09375 to 0.09375
- norm_gain: float32 [4096], P('ch'), may hold values from 0.5 to 1.5
Outputs:
- normed_out: bfloat16 [4096, 32768], P('ch', 'seq')
Inputs may be any that keep to these rules, and one draw needn't show every extreme that they name: `decay_rates`: each mode's decay over the whole sequence lies between 1 and 1024.
All inputs are finite; a program needn't handle non-finite values.
Results may differ from a plain program's by a relative error of at most 0.017.
Values may be sent and summed in bfloat16 or wider, within the bound.
No kernel may reach another device: no remote copies, remote signals or barrier semaphores. Data moves between devices by JAX's collectives and lax.ppermute only.
A program may use at most 64 MiB of HBM per device.

v0:
```python
import functools

import jax
import jax.numpy as jnp
from jax import lax
from jax.experimental import pallas as pl
from jax.experimental.pallas import tpu as pltpu
from jax.sharding import PartitionSpec as P

highest = lax.Precision.HIGHEST
epsilon = 1e-06
block_len = 256
tile_ch = 64


def conv_kernel(x_ref, g_ref, p_ref, o_ref):
    modes = p_ref.shape[1]
    tc, seg = x_ref.shape
    L = block_len
    shape = (modes, tc, L)
    rate = jnp.broadcast_to(p_ref[0][:, :, 0:1], shape)
    weight = jnp.broadcast_to(p_ref[1][:, :, 0:1], shape)
    state = jnp.broadcast_to(p_ref[2][:, :, 0:1], shape)
    pos = lax.broadcasted_iota(jnp.int32, shape, 2).astype(jnp.float32)
    grow = jnp.exp(rate * pos)
    shrink = weight * jnp.exp(-rate * pos)
    step_decay = jnp.exp(-rate)
    block_decay = jnp.exp(-rate * (L - 1.0))
    first = pos == 0.0
    rows = lax.broadcasted_iota(jnp.int32, (L, L), 0)
    cols = lax.broadcasted_iota(jnp.int32, (L, L), 1)
    upper = (rows <= cols).astype(jnp.bfloat16)
    for b in range(seg // L):
        xb = x_ref[:, b * L:(b + 1) * L].astype(jnp.float32)
        u = xb[None] * grow + jnp.where(first, step_decay * state, 0.0)
        u2 = u.reshape(modes * tc, L)
        hi = u2.astype(jnp.bfloat16)
        lo = (u2 - hi.astype(jnp.float32)).astype(jnp.bfloat16)
        pre = jnp.dot(hi, upper, preferred_element_type=jnp.float32) + jnp.dot(
            lo, upper, preferred_element_type=jnp.float32
        )
        pre = pre.reshape(modes, tc, L)
        conv = jnp.sum(shrink * pre, axis=0)
        state = jnp.broadcast_to(pre[:, :, L - 1:L], shape) * block_decay
        gate = g_ref[:, b * L:(b + 1) * L].astype(jnp.float32)
        o_ref[:, b * L:(b + 1) * L] = (gate * conv).astype(o_ref.dtype)


def gated_conv(signal, gate, params):
    rows, seg = signal.shape
    modes = params.shape[1]
    tc = tile_ch
    return pl.pallas_call(
        conv_kernel,
        out_shape=jax.ShapeDtypeStruct((rows, seg), jnp.bfloat16),
        grid=(rows // tc,),
        in_specs=[
            pl.BlockSpec((tc, seg), lambda i: (i, 0)),
            pl.BlockSpec((tc, seg), lambda i: (i, 0)),
            pl.BlockSpec((3, modes, tc, 128), lambda i: (0, 0, i, 0)),
        ],
        out_specs=pl.BlockSpec((tc, seg), lambda i: (i, 0)),
        compiler_params=pltpu.CompilerParams(vmem_limit_bytes=48 * 1024 * 1024),
        cost_estimate=pl.CostEstimate(
            flops=4 * rows * seg * modes * block_len + 12 * rows * seg * modes,
            transcendentals=2 * rows * modes * block_len,
            bytes_accessed=6 * rows * seg + 3 * modes * rows * 128 * 4,
        ),
    )(signal, gate, params)


def local_end_state(signal, rates):
    rows, seg = signal.shape
    L = block_len
    nb = seg // L
    pos = jnp.arange(L, dtype=jnp.float32)
    blocks = signal.astype(jnp.float32).reshape(rows, nb, L)
    tail = jnp.exp(-rates[:, :, None] * (L - 1.0 - pos)[None, None, :])
    per_block = jnp.einsum("cbs,cms->cbm", blocks, tail, precision=highest)
    later = (nb - 1.0 - jnp.arange(nb, dtype=jnp.float32)) * L
    carry = jnp.exp(-rates[:, None, :] * later[None, :, None])
    return jnp.sum(per_block * carry, axis=1)


def per_device(residual_in, key_value, query_gate, decay_rates, residues, out_weight, norm_gain):
    rows, seg_len = key_value.shape
    n_seq = lax.axis_size("seq")
    total_len = n_seq * seg_len
    rates = decay_rates / total_len
    weights = residues * jnp.sqrt(2.0 * rates)
    own_end = local_end_state(key_value, rates)
    ends = lax.all_gather(own_end, "seq")
    me = lax.axis_index("seq")
    others = jnp.arange(n_seq)
    gap = jnp.maximum(me - 1 - others, 0).astype(jnp.float32) * seg_len
    span = jnp.where(
        (others < me)[:, None, None],
        jnp.exp(-rates[None] * gap[:, None, None]),
        0.0,
    )
    carry_in = jnp.sum(span * ends, axis=0)
    packed = jnp.stack([rates.T, weights.T, carry_in.T])
    packed = jnp.broadcast_to(packed[..., None], packed.shape + (128,))
    gated = gated_conv(key_value, query_gate, packed)
    summed = lax.psum_scatter(
        lax.dot_general(
            out_weight, gated, (((0,), (0,)), ((), ())), preferred_element_type=jnp.float32
        ).astype(jnp.bfloat16),
        "ch",
        scatter_dimension=0,
        tiled=True,
    ).astype(jnp.float32)
    mixed = residual_in.astype(jnp.float32) + summed
    squares = lax.psum(jnp.sum(mixed * mixed, axis=0), "ch")
    square_mean = squares / out_weight.shape[1]
    scaled = mixed * lax.rsqrt(square_mean + epsilon)[None, :] * norm_gain[:, None]
    return scaled.astype(jnp.bfloat16)


def solution(mesh):
    placed = (
        P("ch", "seq"),
        P("ch", "seq"),
        P("ch", "seq"),
        P("ch", None),
        P("ch", None),
        P("ch", None),
        P("ch"),
    )
    return jax.shard_map(
        per_device, mesh=mesh, in_specs=placed, out_specs=P("ch", "seq"), check_vma=False
    )
```

profile of v0, /device:TPU:1, one launch (start us, length us, event | category | flops | bytes accessed | tf_op | source)
XLA Modules:
  0.0 235.4 jit_solution(9224261345525385068)
XLA Ops:
  6.5 0.0 all-gather.3.cloned.1.call-start
  6.6 0.8 multiply_bitcast_fusion.1
  7.3 0.1 copy.31
  7.5 1.9 reshape.32
  9.3 7.7 %fusion.11 = f32[512,16]{1,0:T(8,128)} fusion(bf16[512,4,256]{2,1,0:T(4,128)(2,1)S(1)} %reshape.32, f32[256]{0:T(256)S(1)} %iota_subtract_fusion, f32[512,16]{1,0:T(8,128)S(1)} %copy.31, f32[4]{0:T(128)S(1)} %subtract_multiply_fusion), kind=kOutput, calls=%fused_computation.11 | convolution fusion | flops 102850560 | bytes 1115152 | tf_op jit(solution)/shard_map/cbs,cms->cbm/dot_general | solution.py:79
  17.0 0.0 all-gather.3.cloned.1.call-update
  17.1 0.0 reduce-scatter.2.cloned.1.call-start
  17.1 100.9 %all-gather.3.cloned.1.call-done = f32[16384,16]{1,0:T(8,128)} async-done(((f32[512,16]{1,0:T(8,128)}), f32[16384,16]{1,0:T(8,128)}) %all-gather.3.cloned.1.call-update) | async-done | bytes 1048592 | tf_op jit(solution)/shard_map/all_gather | solution.py:92
  118.1 5.2 %copy.36 = f32[32,512,16]{1,0,2:T(8,128)S(1)} copy(f32[32,512,16]{2,1,0:T(8,128)} %bitcast.23) | data formatting | bytes 2097152 | tf_op jit(solution)/shard_map/all_gather | solution.py:92
  123.3 0.3 multiply_reduce_fusion.1
  123.7 0.0 copy-start
  123.7 0.0 copy-start.1
  123.7 7.1 %broadcast_in_dim.16.p_ref = f32[3,16,512,128]{3,2,1,0:T(8,128)} broadcast(f32[3,16,512]{2,1,0:T(8,128)S(1)} %pad_maximum_fusion), dimensions={0,1,2} | broadcast | bytes 12681216 | tf_op jit(solution)/shard_map/broadcast_in_dim | solution.py:103
  130.8 0.0 copy-done
  130.8 20.8 %shard_map.73 = bf16[512,1024]{1,0:T(8,128)(2,1)S(1)} custom-call(bf16[512,1024]{1,0:T(8,128)(2,1)S(1)} %copy-done, bf16[512,1024]{1,0:T(8,128)(2,1)S(1)} %copy-done.1, f32[3,16,512,128]{3,2,1,0:T(8,128)} %broadcast_in_dim.16.p_ref), custom_call_target="tpu_custom_call" | custom-call | flops 8690597888 | bytes 15728640 | tf_op jit(solution)/shard_map/pallas_call | solution.py:53
  151.7 6.8 %convert_bitcast_fusion = bf16[4096,1024]{0,1:T(8,128)(2,1)} fusion(bf16[512,1024]{1,0:T(8,128)(2,1)S(1)} %shard_map.73, bf16[512,4096]{1,0:T(8,128)(2,1)S(1)} %copy-done.4), kind=kOutput, calls=%fused_computation | convolution fusion | flops 4299161600 | bytes 13631488 | tf_op jit(solution)/shard_map/dot_general | solution.py:106
  158.4 0.0 reduce-scatter.2.cloned.1.call-update
  158.5 1.2 copy-done.2
  159.7 0.5 copy.30
  160.2 50.7 %reduce-scatter.2.cloned.1.call-done = bf16[512,1024]{0,1:T(8,128)(2,1)} async-done(((bf16[4096,1024]{0,1:T(8,128)(2,1)}), bf16[512,1024]{0,1:T(8,128)(2,1)}) %reduce-scatter.2.cloned.1.call-update) | async-done | bytes 1048592 | tf_op jit(solution)/shard_map/reduce_scatter | solution.py:105
  210.9 1.6 multiply_reduce_fusion
  212.6 13.0 %psum.7 = f32[1024]{0:T(1024)S(1)} all-reduce(f32[1024]{0:T(1024)S(1)} %multiply_reduce_fusion), channel_id=1, replica_groups=mesh['seq'=32,'ch'=8] {'ch'}, use_global_device_ids=true, to_apply=%region_4.5 | all-reduce | flops 1024 | bytes 8192 | tf_op jit(solution)/shard_map/psum | solution.py:114
  225.6 1.6 multiply_convert_fusion
  227.2 1.3 copy.35
  (12 shorter events, 0.1 us)
Async XLA Ops:
  6.5 111.5 %all-gather.3.cloned.1.call-start = ((), (), s32[]{:S(2)}) async-start(), calls=%async_computation.2 | async-start | bytes 8650752 | tf_op jit(solution)/shard_map/all_gather | solution.py:92
  17.1 193.9 %reduce-scatter.2.cloned.1.call-start = ((), (), s32[]{:S(2)}) async-start(), calls=%async_computation.1 | async-start | bytes 9437184 | tf_op jit(solution)/shard_map/reduce_scatter | solution.py:105
  123.7 7.1 %copy-start = (bf16[512,1024]{1,0:T(8,128)(2,1)S(1)}, bf16[512,1024]{1,0:T(8,128)(2,1)}, u32[]{:S(2)}) copy-start(bf16[512,1024]{1,0:T(8,128)(2,1)} %x_ref.1) | copy-start | bytes 3145732
  123.7 7.1 %copy-start.1 = (bf16[512,1024]{1,0:T(8,128)(2,1)S(1)}, bf16[512,1024]{1,0:T(8,128)(2,1)}, u32[]{:S(2)}) copy-start(bf16[512,1024]{1,0:T(8,128)(2,1)} %g_ref.1) | copy-start | bytes 3145732
  130.8 20.9 %copy-start.4 = (bf16[512,4096]{1,0:T(8,128)(2,1)S(1)}, bf16[512,4096]{1,0:T(8,128)(2,1)}, u32[]{:S(2)}) copy-start(bf16[512,4096]{1,0:T(8,128)(2,1)} %param.12) | copy-start | bytes 12582916
  158.4 1.2 copy-start.2
  159.7 65.9 %copy-start.3 = (f32[512]{0:T(512)S(1)}, f32[512]{0:T(512)}, u32[]{:S(2)}) copy-start(f32[512]{0:T(512)} %param.13) | copy-start | bytes 6148
Sparse Core Ops, SparseCore 0:
  17.2 100.8 all-gather.2
  158.6 52.3 reduce-scatter.1
where the time goes:
time: 236 us; the launch traced here: 235 us
  waiting for transfers between devices  152 us (64%)
  Pallas kernels  20.8 us (9%)
  local copies, waits for them, and re-layouts  17.4 us (7%)
  matrix products  14.4 us (6%)
  between operations  13.5 us (6%)
  blocking collectives  13 us (6%)
  other arithmetic  4.42 us (2%)
    all_gather x1, waiting for transfers between devices, per_device(): ends = lax.all_gather(own_end, 'seq')  101 us
    reduce_scatter x1, waiting for transfers between devices, per_device(): lax.psum_scatter(lax.dot_general(out_weight, gated, (((0,), (0,)), ((), (...  50.7 us
    pallas_call x1, Pallas kernels, gated_conv(): pl.pallas_call(conv_kernel, out_shape=jax.ShapeDtypeStruct((rows, seg), j...  20.8 us
    psum x1, blocking collectives, per_device(): squares = lax.psum(jnp.sum(mixed * mixed, axis=0), 'ch')  13 us
    dot_general x1, matrix products, local_end_state(): per_block = jnp.einsum('cbs,cms->cbm', blocks, tail, precision=highest)  7.69 us
    broadcast_in_dim x1, local copies, waits for them, and re-layouts, per_device(): packed = jnp.broadcast_to(packed[..., None], packed.shape + (128,))  7.12 us
    dot_general x1, matrix products, per_device(): lax.dot_general(out_weight, gated, (((0,), (0,)), ((), ())), preferred_el...  6.75 us
    all_gather x1, local copies, waits for them, and re-layouts, per_device(): ends = lax.all_gather(own_end, 'seq')  5.24 us
  transfers between devices with their start and end apart: 2, of which 2 were waited for; matrix products, arithmetic and copies ran while one was open for 0% of the time, Pallas kernels for 0%

commit v1 on v0

--- a/solution.py
+++ b/solution.py
@@ -14,18 +14,23 @@
 
 
 def conv_kernel(x_ref, g_ref, p_ref, o_ref):
-    modes = p_ref.shape[1]
+    modes = p_ref.shape[0]
     tc, seg = x_ref.shape
     L = block_len
     shape = (modes, tc, L)
-    rate = jnp.broadcast_to(p_ref[0][:, :, 0:1], shape)
-    weight = jnp.broadcast_to(p_ref[1][:, :, 0:1], shape)
-    state = jnp.broadcast_to(p_ref[2][:, :, 0:1], shape)
+    p = p_ref[...]
+    half = (modes, tc, 128)
+    rate_h = jnp.broadcast_to(p[:, :, 0:1], half)
+    step_h = jnp.exp(-rate_h)
+    end_h = jnp.exp(-rate_h * (L - 1.0))
+    rate = jnp.concatenate([rate_h, rate_h], axis=2)
+    weight = jnp.broadcast_to(p[:, :, 1:2], shape)
+    state = jnp.broadcast_to(p[:, :, 2:3], shape)
     pos = lax.broadcasted_iota(jnp.int32, shape, 2).astype(jnp.float32)
     grow = jnp.exp(rate * pos)
     shrink = weight * jnp.exp(-rate * pos)
-    step_decay = jnp.exp(-rate)
-    block_decay = jnp.exp(-rate * (L - 1.0))
+    step_decay = jnp.concatenate([step_h, step_h], axis=2)
+    block_decay = jnp.concatenate([end_h, end_h], axis=2)
     first = pos == 0.0
     rows = lax.broadcasted_iota(jnp.int32, (L, L), 0)
     cols = lax.broadcasted_iota(jnp.int32, (L, L), 1)
@@ -48,7 +53,7 @@
 
 def gated_conv(signal, gate, params):
     rows, seg = signal.shape
-    modes = params.shape[1]
+    modes = params.shape[0]
     tc = tile_ch
     return pl.pallas_call(
         conv_kernel,
@@ -57,29 +62,56 @@
         in_specs=[
             pl.BlockSpec((tc, seg), lambda i: (i, 0)),
             pl.BlockSpec((tc, seg), lambda i: (i, 0)),
-            pl.BlockSpec((3, modes, tc, 128), lambda i: (0, 0, i, 0)),
+            pl.BlockSpec((modes, tc, 128), lambda i: (0, i, 0)),
         ],
         out_specs=pl.BlockSpec((tc, seg), lambda i: (i, 0)),
         compiler_params=pltpu.CompilerParams(vmem_limit_bytes=48 * 1024 * 1024),
         cost_estimate=pl.CostEstimate(
             flops=4 * rows * seg * modes * block_len + 12 * rows * seg * modes,
             transcendentals=2 * rows * modes * block_len,
-            bytes_accessed=6 * rows * seg + 3 * modes * rows * 128 * 4,
+            bytes_accessed=6 * rows * seg + modes * rows * 128 * 4,
         ),
     )(signal, gate, params)
 
 
-def local_end_state(signal, rates):
-    rows, seg = signal.shape
+def end_kernel(x_ref, p_ref, o_ref):
+    modes = p_ref.shape[0]
+    tc, seg = x_ref.shape
     L = block_len
     nb = seg // L
-    pos = jnp.arange(L, dtype=jnp.float32)
-    blocks = signal.astype(jnp.float32).reshape(rows, nb, L)
-    tail = jnp.exp(-rates[:, :, None] * (L - 1.0 - pos)[None, None, :])
-    per_block = jnp.einsum("cbs,cms->cbm", blocks, tail, precision=highest)
-    later = (nb - 1.0 - jnp.arange(nb, dtype=jnp.float32)) * L
-    carry = jnp.exp(-rates[:, None, :] * later[None, :, None])
-    return jnp.sum(per_block * carry, axis=1)
+    shape = (modes, tc, L)
+    rate = jnp.broadcast_to(p_ref[...][:, :, 0:1], shape)
+    pos = lax.broadcasted_iota(jnp.int32, shape, 2).astype(jnp.float32)
+    tail = jnp.exp(-rate * (L - 1.0 - pos))
+    whole = jnp.exp(-rate * float(L))
+    total = jnp.zeros(shape, jnp.float32)
+    for b in range(nb):
+        xb = x_ref[:, b * L:(b + 1) * L].astype(jnp.float32)
+        total = total * whole + xb[None] * tail
+    summed = jnp.sum(total, axis=2, keepdims=True)
+    o_ref[...] = jnp.broadcast_to(summed, (modes, tc, 128))
+
+
+def local_end_state(signal, params):
+    rows, seg = signal.shape
+    modes = params.shape[0]
+    tc = tile_ch
+    return pl.pallas_call(
+        end_kernel,
+        out_shape=jax.ShapeDtypeStruct((modes, rows, 128), jnp.float32),
+        grid=(rows // tc,),
+        in_specs=[
+            pl.BlockSpec((tc, seg), lambda i: (i, 0)),
+            pl.BlockSpec((modes, tc, 128), lambda i: (0, i, 0)),
+        ],
+        out_specs=pl.BlockSpec((modes, tc, 128), lambda i: (0, i, 0)),
+        compiler_params=pltpu.CompilerParams(vmem_limit_bytes=48 * 1024 * 1024),
+        cost_estimate=pl.CostEstimate(
+            flops=3 * rows * seg * modes,
+            transcendentals=rows * seg * modes,
+            bytes_accessed=2 * rows * seg + 2 * modes * rows * 128 * 4,
+        ),
+    )(signal, params)[:, :, 0]
 
 
 def per_device(residual_in, key_value, query_gate, decay_rates, residues, out_weight, norm_gain):
@@ -88,19 +120,21 @@
     total_len = n_seq * seg_len
     rates = decay_rates / total_len
     weights = residues * jnp.sqrt(2.0 * rates)
-    own_end = local_end_state(key_value, rates)
-    ends = lax.all_gather(own_end, "seq")
-    me = lax.axis_index("seq")
-    others = jnp.arange(n_seq)
-    gap = jnp.maximum(me - 1 - others, 0).astype(jnp.float32) * seg_len
-    span = jnp.where(
-        (others < me)[:, None, None],
-        jnp.exp(-rates[None] * gap[:, None, None]),
-        0.0,
+    lanes = lax.broadcasted_iota(jnp.int32, (1, 1, 128), 2)
+    base = jnp.where(lanes == 0, rates.T[:, :, None], 0.0) + jnp.where(
+        lanes == 1, weights.T[:, :, None], 0.0
     )
-    carry_in = jnp.sum(span * ends, axis=0)
-    packed = jnp.stack([rates.T, weights.T, carry_in.T])
-    packed = jnp.broadcast_to(packed[..., None], packed.shape + (128,))
+    own_end = local_end_state(key_value, base)
+    block_decay = jnp.exp(-rates.T * seg_len)
+    carry_in = lax.ppermute(own_end, "seq", [(i, i + 1) for i in range(n_seq - 1)])
+    shift = 1
+    factor = block_decay
+    while shift < n_seq:
+        moved = lax.ppermute(carry_in, "seq", [(i, i + shift) for i in range(n_seq - shift)])
+        carry_in = carry_in + factor * moved
+        factor = factor * factor
+        shift *= 2
+    packed = base + jnp.where(lanes == 2, carry_in[:, :, None], 0.0)
     gated = gated_conv(key_value, query_gate, packed)
     summed = lax.psum_scatter(
         lax.dot_general(

time: 236 us -> 182 us (0.77)
  waiting for transfers between devices: 152 us -> 63.8 us
  starting transfers between devices: 0.04 us -> 37.7 us
  local copies, waits for them, and re-layouts: 17.4 us -> 4.22 us
  other arithmetic: 4.42 us -> 13.7 us
  Pallas kernels: 20.8 us -> 28.6 us
  matrix products: 14.4 us -> 6.78 us
    all_gather x1 -> x0, waiting for transfers between devices: 101 us -> none  [per_device(): ends = lax.all_gather(own_end, 'seq')]
    ppermute x0 -> x6, starting transfers between devices: none -> 37.7 us  [the longest x5 33.3 us: per_device(): lax.ppermute(carry_in, 'seq', [(i, i + shift) for i in range(n_seq - shif...]
    add x0 -> x7, other arithmetic: none -> 9.55 us  [the longest x1 5.64 us: per_device(): packed = base + jnp.where(lanes == 2, carry_in[:, :, None], 0.0)]
    pallas_call x0 -> x1, Pallas kernels: none -> 8.1 us  [local_end_state(): pl.pallas_call(end_kernel, out_shape=jax.ShapeDtypeStruct((modes, rows, 1...]
    dot_general x1 -> x0, matrix products: 7.69 us -> none  [local_end_state(): per_block = jnp.einsum('cbs,cms->cbm', blocks, tail, precision=highest)]
    broadcast_in_dim x1 -> x0, local copies, waits for them, and re-layouts: 7.12 us -> none  [per_device(): packed = jnp.broadcast_to(packed[..., None], packed.shape + (128,))]
    reduce_scatter x1, waiting for transfers between devices: 50.7 us -> 57.8 us  [per_device(): lax.psum_scatter(lax.dot_general(out_weight, gated, (((0,), (0,)), ((), (...]
    ppermute x0 -> x6, waiting for transfers between devices: none -> 6.02 us  [the longest x5 5.01 us: per_device(): lax.ppermute(carry_in, 'seq', [(i, i + shift) for i in range(n_seq - shif...]
  transfers between devices with their start and end apart: 2 -> 7, of which waited for: 2 -> 7; matrix products, arithmetic and copies ran while one was open for 0% -> 0% of each run, Pallas kernels for 0% -> 0%
where the time goes in v1:
time: 182 us; the launch traced here: 181 us
  waiting for transfers between devices  63.8 us (35%)
  starting transfers between devices  37.7 us (21%)
  Pallas kernels  28.6 us (16%)
  other arithmetic  13.7 us (8%)
  between operations  13.5 us (7%)
  blocking collectives  13 us (7%)
  matrix products  6.78 us (4%)
  local copies, waits for them, and re-layouts  4.22 us (2%)
    reduce_scatter x1, waiting for transfers between devices, per_device(): lax.psum_scatter(lax.dot_general(out_weight, gated, (((0,), (0,)), ((), (...  57.8 us
    ppermute x5, starting transfers between devices, per_device(): lax.ppermute(carry_in, 'seq', [(i, i + shift) for i in range(n_seq - shif...  33.3 us
    pallas_call x1, Pallas kernels, gated_conv(): pl.pallas_call(conv_kernel, out_shape=jax.ShapeDtypeStruct((rows, seg), j...  20.5 us
    psum x1, blocking collectives, per_device(): squares = lax.psum(jnp.sum(mixed * mixed, axis=0), 'ch')  13 us
    pallas_call x1, Pallas kernels, local_end_state(): pl.pallas_call(end_kernel, out_shape=jax.ShapeDtypeStruct((modes, rows, 1...  8.1 us
    dot_general x1, matrix products, per_device(): lax.dot_general(out_weight, gated, (((0,), (0,)), ((), ())), preferred_el...  6.78 us
    add x1, other arithmetic, per_device(): packed = base + jnp.where(lanes == 2, carry_in[:, :, None], 0.0)  5.64 us
    ppermute x5, waiting for transfers between devices, per_device(): lax.ppermute(carry_in, 'seq', [(i, i + shift) for i in range(n_seq - shif...  5.01 us
  transfers between devices with their start and end apart: 7, of which 7 were waited for; matrix products, arithmetic and copies ran while one was open for 0% of the time, Pallas kernels for 0%

profile of v1, /device:TPU:1, one launch (start us, length us, event | category | flops | bytes accessed | tf_op | source)
XLA Modules:
  0.0 181.4 jit_solution(4927750922248383131)
XLA Ops:
  7.4 3.8 %select_add_fusion.1.p_ref = f32[16,512,128]{2,1,0:T(8,128)} fusion(f32[16,512]{1,0:T(8,128)S(1)} %get-tuple-element.6, f32[16,512]{1,0:T(8,128)S(1)} %get-tuple-element.5, pred[128]{0:T(512)(128)(4,1)S(1)} %get-tuple-element.7, pred[128]{0:T(512)(128)(4,1)S(1)} %get-tuple-element.8), kind=kLoop, calls=%fused_computation.3 | loop fusion | flops 3145728 | bytes 4260096 | tf_op jit(solution)/shard_map/add | solution.py:124
  11.3 8.1 %shard_map.73 = f32[16,512,128]{2,1,0:T(8,128)S(1)} custom-call(bf16[512,1024]{1,0:T(8,128)(2,1)S(1)} %copy-done, f32[16,512,128]{2,1,0:T(8,128)} %select_add_fusion.1.p_ref), custom_call_target="tpu_custom_call" | custom-call | flops 25165824 | bytes 9437184 | tf_op jit(solution)/shard_map/pallas_call | solution.py:99
  19.4 1.1 slice_reduce_fusion
  20.5 4.4 %collective-permute-start = (f32[16,512]{1,0:T(8,128)S(1)}, f32[16,512]{1,0:T(8,128)S(1)}, u32[]{:S(2)}, u32[]{:S(2)}) collective-permute-start(f32[16,512]{1,0:T(8,128)S(1)} %slice_reduce_fusion), channel_id=1, source_target_pairs={{0,8},{8,16},{16,24},{24,32},{32,40},{40,48},{48,56},{56,64},{64,7... | collective-permute-start | bytes 98312 | tf_op jit(solution)/shard_map/ppermute | solution.py:129
  24.9 1.0 collective-permute-done
  25.9 3.6 %collective-permute-start.1 = (f32[16,512]{1,0:T(8,128)S(1)}, f32[16,512]{1,0:T(8,128)S(1)}, u32[]{:S(2)}, u32[]{:S(2)}) collective-permute-start(f32[16,512]{1,0:T(8,128)S(1)} %collective-permute-done), channel_id=1, source_target_pairs={{0,8},{8,16},{16,24},{24,32},{32,40},{40,48},{48,56},{56,64},{64,7... | collective-permute-start | bytes 98312 | tf_op jit(solution)/shard_map/ppermute | solution.py:133
  29.6 1.0 collective-permute-done.1
  30.6 6.0 %collective-permute-start.2 = (f32[16,512]{1,0:T(8,128)S(1)}, f32[16,512]{1,0:T(8,128)S(1)}, u32[]{:S(2)}, u32[]{:S(2)}) collective-permute-start(f32[16,512]{1,0:T(8,128)S(1)} %multiply_add_fusion.4), channel_id=1, source_target_pairs={{0,16},{8,24},{16,32},{24,40},{32,48},{40,56},{48,64},{56,72},{64,... | collective-permute-start | bytes 98312 | tf_op jit(solution)/shard_map/ppermute | solution.py:133
  36.6 1.0 collective-permute-done.2
  37.6 11.1 %collective-permute-start.3 = (f32[16,512]{1,0:T(8,128)S(1)}, f32[16,512]{1,0:T(8,128)S(1)}, u32[]{:S(2)}, u32[]{:S(2)}) collective-permute-start(f32[16,512]{1,0:T(8,128)S(1)} %multiply_add_fusion.3), channel_id=1, source_target_pairs={{0,32},{8,40},{16,48},{24,56},{32,64},{40,72},{48,80},{56,88},{64,... | collective-permute-start | bytes 98312 | tf_op jit(solution)/shard_map/ppermute | solution.py:133
  48.7 1.0 collective-permute-done.3
  49.8 7.4 %collective-permute-start.4 = (f32[16,512]{1,0:T(8,128)S(1)}, f32[16,512]{1,0:T(8,128)S(1)}, u32[]{:S(2)}, u32[]{:S(2)}) collective-permute-start(f32[16,512]{1,0:T(8,128)S(1)} %multiply_add_fusion.2), channel_id=1, source_target_pairs={{0,64},{8,72},{16,80},{24,88},{32,96},{40,104},{48,112},{56,120},{... | collective-permute-start | bytes 98312 | tf_op jit(solution)/shard_map/ppermute | solution.py:133
  57.2 1.0 collective-permute-done.4
  58.2 5.2 %collective-permute-start.5 = (f32[16,512]{1,0:T(8,128)S(1)}, f32[16,512]{1,0:T(8,128)S(1)}, u32[]{:S(2)}, u32[]{:S(2)}) collective-permute-start(f32[16,512]{1,0:T(8,128)S(1)} %multiply_add_fusion.1), channel_id=1, source_target_pairs={{0,128},{8,136},{16,144},{24,152},{32,160},{40,168},{48,176},{56,1... | collective-permute-start | bytes 98312 | tf_op jit(solution)/shard_map/ppermute | solution.py:133
  63.4 1.0 collective-permute-done.5
  64.4 5.6 %select_add_fusion.p_ref = f32[16,512,128]{2,1,0:T(8,128)} fusion(f32[16,512]{1,0:T(8,128)S(1)} %multiply_add_fusion, pred[128]{0:T(512)(128)(4,1)S(1)} %iota_compare_fusion, f32[16,512]{1,0:T(8,128)S(1)} %get-tuple-element.6, pred[128]{0:T(512)(128)(4,1)S(1)} %get-tuple-element.7, f32[16,512]{1,0:T(8,128)S(1)} %get-tuple-element.5, ...), kind=kLoop, calls=%fused_computation.2 | loop fusion | flops 5242880 | bytes 4292992 | tf_op jit(solution)/shard_map/add | solution.py:137
  70.1 20.5 %shard_map.74 = bf16[512,1024]{1,0:T(8,128)(2,1)S(1)} custom-call(bf16[512,1024]{1,0:T(8,128)(2,1)S(1)} %copy-done, bf16[512,1024]{1,0:T(8,128)(2,1)S(1)} %copy-done.1, f32[16,512,128]{2,1,0:T(8,128)} %select_add_fusion.p_ref), custom_call_target="tpu_custom_call" | custom-call | flops 8690597888 | bytes 7340032 | tf_op jit(solution)/shard_map/pallas_call | solution.py:58
  90.6 6.8 %convert_bitcast_fusion = bf16[4096,1024]{0,1:T(8,128)(2,1)} fusion(bf16[512,1024]{1,0:T(8,128)(2,1)S(1)} %shard_map.74, bf16[512,4096]{1,0:T(8,128)(2,1)S(1)} %copy-done.5), kind=kOutput, calls=%fused_computation | convolution fusion | flops 4299161600 | bytes 13631488 | tf_op jit(solution)/shard_map/dot_general | solution.py:140
  97.4 1.2 copy-done.3
  99.2 57.8 %reduce-scatter.2.cloned.1.call-done = bf16[512,1024]{0,1:T(8,128)(2,1)} async-done(((bf16[4096,1024]{0,1:T(8,128)(2,1)}), bf16[512,1024]{0,1:T(8,128)(2,1)}) %reduce-scatter.2.cloned.1.call-update) | async-done | bytes 1048592 | tf_op jit(solution)/shard_map/reduce_scatter | solution.py:139
  157.0 1.6 multiply_reduce_fusion
  158.6 13.0 %psum.7 = f32[1024]{0:T(1024)S(1)} all-reduce(f32[1024]{0:T(1024)S(1)} %multiply_reduce_fusion), channel_id=1, replica_groups=mesh['seq'=32,'ch'=8] {'ch'}, use_global_device_ids=true, to_apply=%region_2.3 | all-reduce | flops 1024 | bytes 8192 | tf_op jit(solution)/shard_map/psum | solution.py:148
  171.7 1.6 multiply_convert_fusion
  173.3 1.3 copy.11
  (23 shorter events, 1.6 us)
Async XLA Ops:
  6.5 4.7 %copy-start = (bf16[512,1024]{1,0:T(8,128)(2,1)S(1)}, bf16[512,1024]{1,0:T(8,128)(2,1)}, u32[]{:S(2)}) copy-start(bf16[512,1024]{1,0:T(8,128)(2,1)} %x_ref.3) | copy-start | bytes 3145732
  6.5 150.5 %reduce-scatter.2.cloned.1.call-start = ((), (), s32[]{:S(2)}) async-start(), calls=%async_computation.1 | async-start | bytes 9437184 | tf_op jit(solution)/shard_map/reduce_scatter | solution.py:139
  19.4 11.2 %copy-start.2 = (f32[512,16]{0,1:T(8,128)S(1)}, f32[512,16]{0,1:T(8,128)}, u32[]{:S(2)}) copy-start(f32[512,16]{0,1:T(8,128)} %param.10) | copy-start | bytes 98308
  19.4 50.7 %copy-start.1 = (bf16[512,1024]{1,0:T(8,128)(2,1)S(1)}, bf16[512,1024]{1,0:T(8,128)(2,1)}, u32[]{:S(2)}) copy-start(bf16[512,1024]{1,0:T(8,128)(2,1)} %g_ref.1) | copy-start | bytes 3145732
  20.5 5.4 %collective-permute-start = (f32[16,512]{1,0:T(8,128)S(1)}, f32[16,512]{1,0:T(8,128)S(1)}, u32[]{:S(2)}, u32[]{:S(2)}) collective-permute-start(f32[16,512]{1,0:T(8,128)S(1)} %slice_reduce_fusion), channel_id=1, source_target_pairs={{0,8},{8,16},{16,24},{24,32},{32,40},{40,48},{48,56},{56,64},{64,7... | collective-permute-start | bytes 98312 | tf_op jit(solution)/shard_map/ppermute | solution.py:129
  25.9 4.6 %collective-permute-start.1 = (f32[16,512]{1,0:T(8,128)S(1)}, f32[16,512]{1,0:T(8,128)S(1)}, u32[]{:S(2)}, u32[]{:S(2)}) collective-permute-start(f32[16,512]{1,0:T(8,128)S(1)} %collective-permute-done), channel_id=1, source_target_pairs={{0,8},{8,16},{16,24},{24,32},{32,40},{40,48},{48,56},{56,64},{64,7... | collective-permute-start | bytes 98312 | tf_op jit(solution)/shard_map/ppermute | solution.py:133
  30.6 7.0 %collective-permute-start.2 = (f32[16,512]{1,0:T(8,128)S(1)}, f32[16,512]{1,0:T(8,128)S(1)}, u32[]{:S(2)}, u32[]{:S(2)}) collective-permute-start(f32[16,512]{1,0:T(8,128)S(1)} %multiply_add_fusion.4), channel_id=1, source_target_pairs={{0,16},{8,24},{16,32},{24,40},{32,48},{40,56},{48,64},{56,72},{64,... | collective-permute-start | bytes 98312 | tf_op jit(solution)/shard_map/ppermute | solution.py:133
  37.6 12.1 %collective-permute-start.3 = (f32[16,512]{1,0:T(8,128)S(1)}, f32[16,512]{1,0:T(8,128)S(1)}, u32[]{:S(2)}, u32[]{:S(2)}) collective-permute-start(f32[16,512]{1,0:T(8,128)S(1)} %multiply_add_fusion.3), channel_id=1, source_target_pairs={{0,32},{8,40},{16,48},{24,56},{32,64},{40,72},{48,80},{56,88},{64,... | collective-permute-start | bytes 98312 | tf_op jit(solution)/shard_map/ppermute | solution.py:133
  49.8 8.4 %collective-permute-start.4 = (f32[16,512]{1,0:T(8,128)S(1)}, f32[16,512]{1,0:T(8,128)S(1)}, u32[]{:S(2)}, u32[]{:S(2)}) collective-permute-start(f32[16,512]{1,0:T(8,128)S(1)} %multiply_add_fusion.2), channel_id=1, source_target_pairs={{0,64},{8,72},{16,80},{24,88},{32,96},{40,104},{48,112},{56,120},{... | collective-permute-start | bytes 98312 | tf_op jit(solution)/shard_map/ppermute | solution.py:133
  58.2 6.2 %collective-permute-start.5 = (f32[16,512]{1,0:T(8,128)S(1)}, f32[16,512]{1,0:T(8,128)S(1)}, u32[]{:S(2)}, u32[]{:S(2)}) collective-permute-start(f32[16,512]{1,0:T(8,128)S(1)} %multiply_add_fusion.1), channel_id=1, source_target_pairs={{0,128},{8,136},{16,144},{24,152},{32,160},{40,168},{48,176},{56,1... | collective-permute-start | bytes 98312 | tf_op jit(solution)/shard_map/ppermute | solution.py:133
  70.1 20.6 %copy-start.5 = (bf16[512,4096]{1,0:T(8,128)(2,1)S(1)}, bf16[512,4096]{1,0:T(8,128)(2,1)}, u32[]{:S(2)}) copy-start(bf16[512,4096]{1,0:T(8,128)(2,1)} %param.12) | copy-start | bytes 12582916
  97.4 1.2 copy-start.3
  98.6 73.0 %copy-start.4 = (f32[512]{0:T(512)S(1)}, f32[512]{0:T(512)}, u32[]{:S(2)}) copy-start(f32[512]{0:T(512)} %param.13) | copy-start | bytes 6148
Sparse Core Ops, SparseCore 0:
  97.6 59.3 reduce-scatter.1
